TPU v7x, 512 devices: a whole 4x4x16 slice. The times are simulated.
512 devices in a mesh: tm: 32 (over z, core), band: 4 (over y), fsdp: 4 (over x).
Axes of the slice: x: 4, y: 4, z: 16, core: 2. Of those that a mesh axis runs over, the one named last changes fastest.
Arguments:
- video: bfloat16 [128, 64, 128, 256], P('tm', 'band', 'fsdp'), may hold values from -8 to 8
- clip_lengths: int32 [16], replicated, may hold values from 1 to 31, 128 in all
- norm_gains: float32 [2, 256], replicated, may hold values from 0.1 to 1.9
- spatial_kernel_weight: bfloat16 [256, 2304], P(('band', 'fsdp')), may hold values from -0.125 to 0.125
- w_time: bfloat16 [256, 768], P(('band', 'fsdp')), may hold values from -0.21875 to 0.21875
- w_qkv: bfloat16 [256, 768], P(('band', 'fsdp')), may hold values from -4 to 4
- w_out: bfloat16 [256, 256], P(('band', 'fsdp')), may hold values from -0.375 to 0.375
Outputs:
- mixed: bfloat16 [4, 4, 512, 128, 256], P('band', 'fsdp', 'tm')
Inputs may be any that keep to these rules, and one draw needn't show every extreme that they name: `clip_lengths`: every clip has at least one frame and the lengths sum to 128.
All inputs are finite; a program needn't handle non-finite values.
Results may differ from a plain program's by a relative error of at most 0.0064.
Values may be sent and summed in bfloat16 or wider, within the bound.
No kernel may reach another device: no remote copies, remote signals or barrier semaphores. Data moves between devices by JAX's collectives and lax.ppermute only.
A program may use at most 64 MiB of HBM per device.

v0:
```python
import math
import jax
import jax.numpy as jnp
from jax import lax
from jax.sharding import PartitionSpec as P

GROUPS = 32
EPS = 1e-06


def with_halo(x, sides, width):
    for axis, dim in sides:
        size, length = (lax.axis_size(axis), x.shape[dim])
        up = [(i, (i + 1) % size) for i in range(size - 1)]
        down = [(j, i) for i, j in up]
        last = lax.slice_in_dim(x, length - width, length, axis=dim)
        initial = lax.slice_in_dim(x, 0, width, axis=dim)
        before = lax.ppermute(last, axis, up)
        after = lax.ppermute(initial, axis, down)
        x = jnp.concatenate([before, x, after], axis=dim)
    return x


def from_behind(x, axis, by):
    length = lax.axis_size(axis)
    pairs = [(i, i + by) for i in range(length) if 0 <= i + by < length]
    return lax.ppermute(x, axis, pairs)


def butterfly_sum(x, axes):
    for axis in axes:
        size = lax.axis_size(axis)
        step = 1
        while step < size:
            pairs = [(i, i ^ step) for i in range(size)]
            x = x + lax.ppermute(x, axis, pairs)
            step *= 2
    return x


def frame_starts(clip_lengths, total):
    ends = jnp.cumsum(clip_lengths)
    begins = ends - clip_lengths
    index = jnp.arange(total, dtype=jnp.int32)
    chosen = jnp.where(begins[None, :] <= index[:, None], begins[None, :], 0)
    return jnp.max(chosen, axis=1)


def group_moments(field):
    frames, height, width, chans = field.shape
    group_width = chans // GROUPS
    vals = field.astype(jnp.float32).reshape(frames, height * width, GROUPS, group_width)
    sums = jnp.sum(vals, axis=(1, 3))
    squares = jnp.sum(vals * vals, axis=(1, 3))
    both = butterfly_sum(jnp.stack([sums, squares]), ("band", "fsdp"))
    sums, squares = (both[0], both[1])
    count = height * width * group_width * lax.axis_size("band") * lax.axis_size("fsdp")
    mean = sums / count
    scale = lax.rsqrt(squares / count - mean * mean + EPS)
    return (mean, scale)


def apply_norm(field, mean, scale, gain):
    shape = field.shape
    chans = shape[-1]
    group_width = chans // GROUPS
    vals = field.astype(jnp.float32).reshape(shape[0], -1, GROUPS, group_width)
    normed = (vals - mean[:, None, :, None]) * scale[:, None, :, None]
    return normed.reshape(shape) * gain


def body(video, clip_lengths, norm_gains, spatial_kernel_weight, w_time, w_qkv, w_out):
    frames, height, width, chans = video.shape
    widths = [w.shape[1] for w in (spatial_kernel_weight, w_time, w_qkv, w_out)]
    packed = jnp.concatenate([spatial_kernel_weight, w_time, w_qkv, w_out], axis=1)
    gathered = lax.all_gather(packed, ("band", "fsdp"), axis=0, tiled=True)
    offsets = [sum(widths[:i]) for i in range(4)]
    space_full, time_full, qkv_full, output_complete = [
        gathered[:, o : o + w] for o, w in zip(offsets, widths)
    ]
    ranks = lax.axis_size("tm")
    total_frames = frames * ranks
    first = lax.axis_index("tm") * frames
    starts = frame_starts(clip_lengths, total_frames)
    local_starts = lax.dynamic_slice_in_dim(starts, first, frames)
    mean_one, scale_one = group_moments(video)
    act = jax.nn.silu(apply_norm(video, mean_one, scale_one, norm_gains[0])).astype(jnp.bfloat16)
    padded = with_halo(act, (("band", 1), ("fsdp", 2)), 1)
    spatial = jnp.zeros((frames, height, width, chans), jnp.float32)
    for tap in range(9):
        shift_y = tap // 3
        shift_x = tap % 3
        spatial = spatial + jnp.einsum(
            "fhwc,cd->fhwd",
            padded[:, shift_y : shift_y + height, shift_x : shift_x + width],
            space_full[:, tap * chans : (tap + 1) * chans],
            preferred_element_type=jnp.float32,
        )
    spatial = spatial.astype(jnp.bfloat16)
    carried = from_behind(spatial[frames - 2 :], "tm", 1)
    extended = jnp.concatenate([carried, spatial], axis=0)
    position = first + jnp.arange(frames, dtype=jnp.int32)
    slots = jnp.arange(frames + 2, dtype=jnp.int32)
    temporal = jnp.zeros((frames, height, width, chans), jnp.float32)
    for tap in range(3):
        source = jnp.maximum(position - 2 + tap, local_starts) - first + 2
        select = (source[:, None] == slots[None, :]).astype(jnp.bfloat16)
        picked = jnp.einsum(
            "fe,ehwc->fhwc", select, extended, preferred_element_type=jnp.float32
        ).astype(jnp.bfloat16)
        temporal = temporal + jnp.einsum(
            "fhwc,cd->fhwd",
            picked,
            time_full[:, tap * chans : (tap + 1) * chans],
            preferred_element_type=jnp.float32,
        )
    resid = (video.astype(jnp.float32) + temporal).astype(jnp.bfloat16)
    pixels = height * width
    group_pixels = pixels // ranks
    flat_resid = resid.reshape(frames, ranks, group_pixels, chans).transpose(1, 0, 2, 3)
    received = lax.all_to_all(flat_resid, "tm", split_axis=0, concat_axis=0, tiled=True)
    resid_time = received.reshape(total_frames, group_pixels, chans)
    mean_two, scale_two = group_moments(resid)
    mine = jnp.concatenate([mean_two, scale_two], axis=1)
    big = jnp.pad(mine, ((0, 8 - frames), (0, 1024 - 2 * GROUPS)))
    moments = lax.all_gather(big, "tm", axis=0, tiled=True).reshape(ranks, 8, 1024)[
        :, :frames, : 2 * GROUPS
    ]
    moments = moments.reshape(total_frames, 2 * GROUPS)
    mean_all, scale_all = (moments[:, :GROUPS], moments[:, GROUPS:])
    flat_norm = apply_norm(resid_time, mean_all, scale_all, norm_gains[1]).astype(jnp.bfloat16)
    qkv_time = jnp.einsum(
        "fpc,cd->fpd", flat_norm, qkv_full, preferred_element_type=jnp.float32
    ).astype(jnp.bfloat16)
    query = qkv_time[..., :chans]
    keys = qkv_time[..., chans : 2 * chans]
    value_rows = qkv_time[..., 2 * chans :]
    index = jnp.arange(total_frames, dtype=jnp.int32)
    allowed = (index[None, :] <= index[:, None]) & (index[None, :] >= starts[:, None])
    scores = jnp.einsum(
        "fpc,gpc->pfg", query, keys, preferred_element_type=jnp.float32
    ) / math.sqrt(chans)
    scores = jnp.where(allowed[None], scores, -1e30)
    top = jnp.max(scores, axis=-1, keepdims=True)
    expo = jnp.where(allowed[None], jnp.exp(scores - top), 0.0)
    attention_probabilities = (expo / jnp.sum(expo, axis=-1, keepdims=True)).astype(jnp.bfloat16)
    attention_output = jnp.einsum(
        "boh,hba->boa", attention_probabilities, value_rows, preferred_element_type=jnp.float32
    ).astype(jnp.bfloat16)
    projected_output = jnp.einsum(
        "axi,iy->axy", attention_output, output_complete, preferred_element_type=jnp.float32
    )
    mixed = (jnp.swapaxes(resid_time, 0, 1).astype(jnp.float32) + projected_output).astype(
        jnp.bfloat16
    )
    return mixed.reshape(1, 1, mixed.shape[0], total_frames, chans)


def solution(mesh):
    return jax.shard_map(
        body,
        mesh=mesh,
        in_specs=(
            P("tm", "band", "fsdp", None),
            P(),
            P(),
            P(("band", "fsdp"), None),
            P(("band", "fsdp"), None),
            P(("band", "fsdp"), None),
            P(("band", "fsdp"), None),
        ),
        out_specs=P("band", "fsdp", "tm", None, None),
        check_vma=False,
    )
```

profile of v0, /device:TPU:1, one launch (start us, length us, event | category | flops | bytes accessed | tf_op | source)
XLA Modules:
  0.0 233.3 jit_solution(3845554850148898094)
XLA Ops:
  6.5 1.7 pad_maximum_fusion.2
  8.3 1.5 convert_reduce_fusion
  10.2 4.0 %collective-permute-start = (f32[2,4,32]{2,1,0:T(4,128)S(1)}, f32[2,4,32]{2,1,0:T(4,128)S(1)}, u32[]{:S(2)}, u32[]{:S(2)}) collective-permute-start(f32[2,4,32]{2,1,0:T(4,128)S(1)} %pad_maximum_fusion.6), channel_id=1, source_target_pairs={{0,4},{4,0},{8,12},{12,8},{1,5},{5,1},{9,13},{13,9},{2,6},{6,2},{1... | collective-permute-start | bytes 3080 | tf_op jit(solution)/shard_map/ppermute | solution.py:36
  14.2 1.0 collective-permute-done
  15.2 5.0 %collective-permute-start.1 = (f32[2,4,32]{2,1,0:T(4,128)S(1)}, f32[2,4,32]{2,1,0:T(4,128)S(1)}, u32[]{:S(2)}, u32[]{:S(2)}) collective-permute-start(f32[2,4,32]{2,1,0:T(4,128)S(1)} %fusion.93), channel_id=1, source_target_pairs={{0,8},{4,12},{8,0},{12,4},{1,9},{5,13},{9,1},{13,5},{2,10},{6,14},... | collective-permute-start | bytes 3080 | tf_op jit(solution)/shard_map/ppermute | solution.py:36
  20.2 1.0 collective-permute-done.1
  21.2 3.2 %collective-permute-start.2 = (f32[2,4,32]{2,1,0:T(4,128)S(1)}, f32[2,4,32]{2,1,0:T(4,128)S(1)}, u32[]{:S(2)}, u32[]{:S(2)}) collective-permute-start(f32[2,4,32]{2,1,0:T(4,128)S(1)} %fusion.104), channel_id=1, source_target_pairs={{0,1},{1,0},{2,3},{3,2},{4,5},{5,4},{6,7},{7,6},{8,9},{9,8},{10,11... | collective-permute-start | bytes 3080 | tf_op jit(solution)/shard_map/ppermute | solution.py:36
  24.3 1.2 collective-permute-done.2
  25.5 4.7 %collective-permute-start.3 = (f32[2,4,32]{2,1,0:T(4,128)S(1)}, f32[2,4,32]{2,1,0:T(4,128)S(1)}, u32[]{:S(2)}, u32[]{:S(2)}) collective-permute-start(f32[2,4,32]{2,1,0:T(4,128)S(1)} %add.111), channel_id=1, source_target_pairs={{0,2},{1,3},{2,0},{3,1},{4,6},{5,7},{6,4},{7,5},{8,10},{9,11},{10,... | collective-permute-start | bytes 3080 | tf_op jit(solution)/shard_map/ppermute | solution.py:36
  30.2 0.8 fusion.96
  31.8 0.7 fusion.16
  32.4 3.2 %collective-permute-start.4 = (bf16[4,1,32,256]{3,2,1,0:T(8,128)(2,1)S(1)}, bf16[4,1,32,256]{3,2,1,0:T(8,128)(2,1)S(1)}, u32[]{:S(2)}, u32[]{:S(2)}) collective-permute-start(bf16[4,1,32,256]{3,2,1,0:T(8,128)(2,1)S(1)} %get-tuple-element.13), channel_id=1, source_target_pairs={{0,4},{4,8},{8,12},{1,5},{5,9},{9,13},{2,6},{6,10},{10,14},{3,7},{... | collective-permute-start | bytes 196616 | tf_op jit(solution)/shard_map/ppermute | solution.py:18
  35.7 1.3 collective-permute-start.5
  37.0 4.1 %collective-permute-done.5 = bf16[4,1,32,256]{3,2,1,0:T(8,128)(2,1)S(1)} collective-permute-done((bf16[4,1,32,256]{3,2,1,0:T(8,128)(2,1)S(1)}, bf16[4,1,32,256]{3,2,1,0:T(8,128)(2,1)S(1)}, u32[]{:S(2)}, u32[]{:S(2)}) %collective-permute-start.5) | collective-permute-done | bytes 65568 | tf_op jit(solution)/shard_map/ppermute | solution.py:19
  41.3 3.2 %collective-permute-start.6 = (bf16[4,18,1,256]{3,2,1,0:T(2,128)(2,1)S(1)}, bf16[4,18,1,256]{3,2,1,0:T(2,128)(2,1)S(1)}, u32[]{:S(2)}, u32[]{:S(2)}) collective-permute-start(bf16[4,18,1,256]{3,2,1,0:T(2,128)(2,1)S(1)} %get-tuple-element.12), channel_id=1, source_target_pairs={{0,1},{1,2},{2,3},{4,5},{5,6},{6,7},{8,9},{9,10},{10,11},{12,13},{... | collective-permute-start | bytes 110600 | tf_op jit(solution)/shard_map/ppermute | solution.py:18
  44.5 1.3 collective-permute-start.7
  45.9 3.7 %collective-permute-done.7 = bf16[4,18,1,256]{3,2,1,0:T(2,128)(2,1)S(1)} collective-permute-done((bf16[4,18,1,256]{3,2,1,0:T(2,128)(2,1)S(1)}, bf16[4,18,1,256]{3,2,1,0:T(2,128)(2,1)S(1)}, u32[]{:S(2)}, u32[]{:S(2)}) %collective-permute-start.7) | collective-permute-done | bytes 36896 | tf_op jit(solution)/shard_map/ppermute | solution.py:19
  49.6 1.8 pad_maximum_fusion.1
  51.3 23.3 %all-gather.3.cloned.1.call-done = bf16[256,4096]{1,0:T(8,128)(2,1)} async-done(((bf16[16,4096]{1,0:T(8,128)(2,1)}), bf16[256,4096]{1,0:T(8,128)(2,1)}) %all-gather.3.cloned.1.call-update) | async-done | bytes 2097168 | tf_op jit(solution)/shard_map/all_gather | solution.py:76
  74.7 1.5 fusion.51
  76.3 0.4 fusion.55
  76.8 0.9 copy-done
  78.6 0.4 fusion.49
  80.4 1.1 add_convert_fusion
  81.5 5.3 %collective-permute-start.8 = (bf16[2,16,32,256]{3,2,1,0:T(8,128)(2,1)S(1)}, bf16[2,16,32,256]{3,2,1,0:T(8,128)(2,1)S(1)}, u32[]{:S(2)}, u32[]{:S(2)}) collective-permute-start(bf16[2,16,32,256]{3,2,1,0:T(8,128)(2,1)S(1)} %slice.197), channel_id=1, source_target_pairs={{0,16},{16,32},{32,48},{48,64},{64,80},{80,96},{96,112},{112,128},... | collective-permute-start | bytes 1572872 | tf_op jit(solution)/shard_map/ppermute | solution.py:27
  87.2 5.7 %collective-permute-done.8 = bf16[2,16,32,256]{3,2,1,0:T(8,128)(2,1)S(1)} collective-permute-done((bf16[2,16,32,256]{3,2,1,0:T(8,128)(2,1)S(1)}, bf16[2,16,32,256]{3,2,1,0:T(8,128)(2,1)S(1)}, u32[]{:S(2)}, u32[]{:S(2)}) %collective-permute-start.8) | collective-permute-done | bytes 524320 | tf_op jit(solution)/shard_map/ppermute | solution.py:27
  93.0 1.2 fusion.22
  94.2 1.2 fusion.19
  95.4 1.2 fusion.25
  96.6 1.3 fusion.60
  98.0 1.4 fusion.62
  99.4 1.7 convert_reduce_fusion.1
  101.2 1.1 copy.89
  102.3 15.1 %all-to-all-start = ((bf16[32,4,16,256]{3,2,1,0:T(8,128)(2,1)}), bf16[32,4,16,256]{3,2,1,0:T(8,128)(2,1)S(1)}, u32[]{:S(2)}, u32[]{:S(2)}) async-start(bf16[32,4,16,256]{3,2,1,0:T(8,128)(2,1)} %bitcast.135), calls=%async_computation | async-start | bytes 2097152 | tf_op jit(solution)/shard_map/all_to_all | solution.py:121
  117.8 2.8 %collective-permute-start.9 = (f32[2,4,32]{2,1,0:T(4,128)S(1)}, f32[2,4,32]{2,1,0:T(4,128)S(1)}, u32[]{:S(2)}, u32[]{:S(2)}) collective-permute-start(f32[2,4,32]{2,1,0:T(4,128)S(1)} %pad_maximum_fusion.7), channel_id=1, source_target_pairs={{0,4},{4,0},{8,12},{12,8},{1,5},{5,1},{9,13},{13,9},{2,6},{6,2},{1... | collective-permute-start | bytes 3080 | tf_op jit(solution)/shard_map/ppermute | solution.py:36
  120.6 1.8 collective-permute-done.9
  122.5 3.7 %collective-permute-start.10 = (f32[2,4,32]{2,1,0:T(4,128)S(1)}, f32[2,4,32]{2,1,0:T(4,128)S(1)}, u32[]{:S(2)}, u32[]{:S(2)}) collective-permute-start(f32[2,4,32]{2,1,0:T(4,128)S(1)} %fusion.92), channel_id=1, source_target_pairs={{0,8},{4,12},{8,0},{12,4},{1,9},{5,13},{9,1},{13,5},{2,10},{6,14},... | collective-permute-start | bytes 3080 | tf_op jit(solution)/shard_map/ppermute | solution.py:36
  126.2 2.4 %collective-permute-done.10 = f32[2,4,32]{2,1,0:T(4,128)S(1)} collective-permute-done((f32[2,4,32]{2,1,0:T(4,128)S(1)}, f32[2,4,32]{2,1,0:T(4,128)S(1)}, u32[]{:S(2)}, u32[]{:S(2)}) %collective-permute-start.10) | collective-permute-done | bytes 1056 | tf_op jit(solution)/shard_map/ppermute | solution.py:36
  128.6 2.8 %collective-permute-start.11 = (f32[2,4,32]{2,1,0:T(4,128)S(1)}, f32[2,4,32]{2,1,0:T(4,128)S(1)}, u32[]{:S(2)}, u32[]{:S(2)}) collective-permute-start(f32[2,4,32]{2,1,0:T(4,128)S(1)} %fusion.103), channel_id=1, source_target_pairs={{0,1},{1,0},{2,3},{3,2},{4,5},{5,4},{6,7},{7,6},{8,9},{9,8},{10,11... | collective-permute-start | bytes 3080 | tf_op jit(solution)/shard_map/ppermute | solution.py:36
  131.4 1.8 collective-permute-done.11
  133.2 3.7 %collective-permute-start.12 = (f32[2,4,32]{2,1,0:T(4,128)S(1)}, f32[2,4,32]{2,1,0:T(4,128)S(1)}, u32[]{:S(2)}, u32[]{:S(2)}) collective-permute-start(f32[2,4,32]{2,1,0:T(4,128)S(1)} %add.132), channel_id=1, source_target_pairs={{0,2},{1,3},{2,0},{3,1},{4,6},{5,7},{6,4},{7,5},{8,10},{9,11},{10,... | collective-permute-start | bytes 3080 | tf_op jit(solution)/shard_map/ppermute | solution.py:36
  137.0 2.4 %collective-permute-done.12 = f32[2,4,32]{2,1,0:T(4,128)S(1)} collective-permute-done((f32[2,4,32]{2,1,0:T(4,128)S(1)}, f32[2,4,32]{2,1,0:T(4,128)S(1)}, u32[]{:S(2)}, u32[]{:S(2)}) %collective-permute-start.12) | collective-permute-done | bytes 1056 | tf_op jit(solution)/shard_map/ppermute | solution.py:36
  139.4 0.7 select_maximum_fusion
  140.1 73.9 %all-gather.5.cloned.1.call-done = f32[256,1024]{1,0:T(8,128)} async-done(((f32[8,1024]{1,0:T(8,128)}), f32[256,1024]{1,0:T(8,128)}) %all-gather.5.cloned.1.call-update) | async-done | bytes 1048592 | tf_op jit(solution)/shard_map/all_gather | solution.py:126
  214.0 0.9 slice.203
  215.8 4.6 %convolution_convert_fusion = bf16[128,16,768]{2,0,1:T(8,128)(2,1)} fusion(f32[128,16,256]{2,1,0:T(8,128)S(1)} %bitcast_convert_fusion, f32[256]{0:T(256)S(1)} %bitcast.150, f32[128,256]{1,0:T(8,128)S(1)} %copy.42, f32[128,256]{1,0:T(8,128)S(1)} %copy.40, bf16[256,4096]{1,0:T(8,128)(2,1)} %all-gather.3.cloned.1.call-done), kind=kOutput, calls=%fused_computation.7 | convolution fusion | flops 808976384 | bytes 5899264 | tf_op jit(solution)/shard_map/fpc,cd->fpd/dot_general | solution.py:132
  220.4 2.1 fusion.97
  222.5 3.9 %fusion.31 = bf16[1,1,16,128,256]{4,3,2,1,0:T(8,128)(2,1)} fusion(f32[128,16,256]{2,1,0:T(8,128)S(1)} %bitcast_convert_fusion, bf16[128,16,768]{2,0,1:T(8,128)(2,1)} %convolution_convert_fusion, f32[16,128,128]{1,2,0:T(8,128)S(1)} %get-tuple-element.24, f32[16,128]{1,0:T(8,128)S(1)} %get-tuple-element.23, bf16[256,4096]{1,0:T(8,128)(2,1)} %all-gather.3.cloned.1.call-done), kind=kOutput, calls=%fused_computation.39 | convolution fusion | flops 404750336 | bytes 5382144 | tf_op jit(solution)/shard_map/axi,iy->axy/dot_general | solution.py:150
  (67 shorter events, 5.7 us)
Async XLA Ops:
  6.5 25.2 %copy-start.1 = (bf16[4,16,32,256]{3,2,1,0:T(8,128)(2,1)S(1)}, bf16[4,16,32,256]{3,2,1,0:T(8,128)(2,1)}, u32[]{:S(2)}) copy-start(bf16[4,16,32,256]{3,2,1,0:T(8,128)(2,1)} %param.7) | copy-start | bytes 3145732
  6.5 68.1 %all-gather.3.cloned.1.call-start = ((), (), s32[]{:S(2)}) async-start(), calls=%async_computation.1 | async-start | bytes 2228224 | tf_op jit(solution)/shard_map/all_gather | solution.py:76
  10.2 5.0 %collective-permute-start = (f32[2,4,32]{2,1,0:T(4,128)S(1)}, f32[2,4,32]{2,1,0:T(4,128)S(1)}, u32[]{:S(2)}, u32[]{:S(2)}) collective-permute-start(f32[2,4,32]{2,1,0:T(4,128)S(1)} %pad_maximum_fusion.6), channel_id=1, source_target_pairs={{0,4},{4,0},{8,12},{12,8},{1,5},{5,1},{9,13},{13,9},{2,6},{6,2},{1... | collective-permute-start | bytes 3080 | tf_op jit(solution)/shard_map/ppermute | solution.py:36
  15.2 6.0 %collective-permute-start.1 = (f32[2,4,32]{2,1,0:T(4,128)S(1)}, f32[2,4,32]{2,1,0:T(4,128)S(1)}, u32[]{:S(2)}, u32[]{:S(2)}) collective-permute-start(f32[2,4,32]{2,1,0:T(4,128)S(1)} %fusion.93), channel_id=1, source_target_pairs={{0,8},{4,12},{8,0},{12,4},{1,9},{5,13},{9,1},{13,5},{2,10},{6,14},... | collective-permute-start | bytes 3080 | tf_op jit(solution)/shard_map/ppermute | solution.py:36
  21.2 4.3 %collective-permute-start.2 = (f32[2,4,32]{2,1,0:T(4,128)S(1)}, f32[2,4,32]{2,1,0:T(4,128)S(1)}, u32[]{:S(2)}, u32[]{:S(2)}) collective-permute-start(f32[2,4,32]{2,1,0:T(4,128)S(1)} %fusion.104), channel_id=1, source_target_pairs={{0,1},{1,0},{2,3},{3,2},{4,5},{5,4},{6,7},{7,6},{8,9},{9,8},{10,11... | collective-permute-start | bytes 3080 | tf_op jit(solution)/shard_map/ppermute | solution.py:36
  25.5 5.8 %collective-permute-start.3 = (f32[2,4,32]{2,1,0:T(4,128)S(1)}, f32[2,4,32]{2,1,0:T(4,128)S(1)}, u32[]{:S(2)}, u32[]{:S(2)}) collective-permute-start(f32[2,4,32]{2,1,0:T(4,128)S(1)} %add.111), channel_id=1, source_target_pairs={{0,2},{1,3},{2,0},{3,1},{4,6},{5,7},{6,4},{7,5},{8,10},{9,11},{10,... | collective-permute-start | bytes 3080 | tf_op jit(solution)/shard_map/ppermute | solution.py:36
  32.4 4.6 %collective-permute-start.4 = (bf16[4,1,32,256]{3,2,1,0:T(8,128)(2,1)S(1)}, bf16[4,1,32,256]{3,2,1,0:T(8,128)(2,1)S(1)}, u32[]{:S(2)}, u32[]{:S(2)}) collective-permute-start(bf16[4,1,32,256]{3,2,1,0:T(8,128)(2,1)S(1)} %get-tuple-element.13), channel_id=1, source_target_pairs={{0,4},{4,8},{8,12},{1,5},{5,9},{9,13},{2,6},{6,10},{10,14},{3,7},{... | collective-permute-start | bytes 196616 | tf_op jit(solution)/shard_map/ppermute | solution.py:18
  35.7 5.4 %collective-permute-start.5 = (bf16[4,1,32,256]{3,2,1,0:T(8,128)(2,1)S(1)}, bf16[4,1,32,256]{3,2,1,0:T(8,128)(2,1)S(1)}, u32[]{:S(2)}, u32[]{:S(2)}) collective-permute-start(bf16[4,1,32,256]{3,2,1,0:T(8,128)(2,1)S(1)} %get-tuple-element.14), channel_id=1, source_target_pairs={{4,0},{8,4},{12,8},{5,1},{9,5},{13,9},{6,2},{10,6},{14,10},{7,3},{... | collective-permute-start | bytes 196616 | tf_op jit(solution)/shard_map/ppermute | solution.py:19
  41.3 4.6 %collective-permute-start.6 = (bf16[4,18,1,256]{3,2,1,0:T(2,128)(2,1)S(1)}, bf16[4,18,1,256]{3,2,1,0:T(2,128)(2,1)S(1)}, u32[]{:S(2)}, u32[]{:S(2)}) collective-permute-start(bf16[4,18,1,256]{3,2,1,0:T(2,128)(2,1)S(1)} %get-tuple-element.12), channel_id=1, source_target_pairs={{0,1},{1,2},{2,3},{4,5},{5,6},{6,7},{8,9},{9,10},{10,11},{12,13},{... | collective-permute-start | bytes 110600 | tf_op jit(solution)/shard_map/ppermute | solution.py:18
  44.5 5.1 %collective-permute-start.7 = (bf16[4,18,1,256]{3,2,1,0:T(2,128)(2,1)S(1)}, bf16[4,18,1,256]{3,2,1,0:T(2,128)(2,1)S(1)}, u32[]{:S(2)}, u32[]{:S(2)}) collective-permute-start(bf16[4,18,1,256]{3,2,1,0:T(2,128)(2,1)S(1)} %get-tuple-element.11), channel_id=1, source_target_pairs={{1,0},{2,1},{3,2},{5,4},{6,5},{7,6},{9,8},{10,9},{11,10},{13,12},{... | collective-permute-start | bytes 110600 | tf_op jit(solution)/shard_map/ppermute | solution.py:19
  74.6 1.7 copy-start.3
  76.3 1.4 copy-start
  80.4 6.4 %copy-start.4 = (s32[16]{0:T(128)S(1)}, s32[16]{0:T(128)}, u32[]{:S(2)}) copy-start(s32[16]{0:T(128)} %param.8) | copy-start | bytes 196
  81.5 11.4 %collective-permute-start.8 = (bf16[2,16,32,256]{3,2,1,0:T(8,128)(2,1)S(1)}, bf16[2,16,32,256]{3,2,1,0:T(8,128)(2,1)S(1)}, u32[]{:S(2)}, u32[]{:S(2)}) collective-permute-start(bf16[2,16,32,256]{3,2,1,0:T(8,128)(2,1)S(1)} %slice.197), channel_id=1, source_target_pairs={{0,16},{16,32},{32,48},{48,64},{64,80},{80,96},{96,112},{112,128},... | collective-permute-start | bytes 1572872 | tf_op jit(solution)/shard_map/ppermute | solution.py:27
  98.0 1.4 copy-start.2
  102.3 113.1 %all-to-all-start = ((bf16[32,4,16,256]{3,2,1,0:T(8,128)(2,1)}), bf16[32,4,16,256]{3,2,1,0:T(8,128)(2,1)S(1)}, u32[]{:S(2)}, u32[]{:S(2)}) async-start(bf16[32,4,16,256]{3,2,1,0:T(8,128)(2,1)} %bitcast.135), calls=%async_computation | async-start | bytes 2097152 | tf_op jit(solution)/shard_map/all_to_all | solution.py:121
  117.4 96.7 %all-gather.5.cloned.1.call-start = ((), (), s32[]{:S(2)}) async-start(), calls=%async_computation.2 | async-start | bytes 1081344 | tf_op jit(solution)/shard_map/all_gather | solution.py:126
  117.8 4.6 %collective-permute-start.9 = (f32[2,4,32]{2,1,0:T(4,128)S(1)}, f32[2,4,32]{2,1,0:T(4,128)S(1)}, u32[]{:S(2)}, u32[]{:S(2)}) collective-permute-start(f32[2,4,32]{2,1,0:T(4,128)S(1)} %pad_maximum_fusion.7), channel_id=1, source_target_pairs={{0,4},{4,0},{8,12},{12,8},{1,5},{5,1},{9,13},{13,9},{2,6},{6,2},{1... | collective-permute-start | bytes 3080 | tf_op jit(solution)/shard_map/ppermute | solution.py:36
  122.5 6.1 %collective-permute-start.10 = (f32[2,4,32]{2,1,0:T(4,128)S(1)}, f32[2,4,32]{2,1,0:T(4,128)S(1)}, u32[]{:S(2)}, u32[]{:S(2)}) collective-permute-start(f32[2,4,32]{2,1,0:T(4,128)S(1)} %fusion.92), channel_id=1, source_target_pairs={{0,8},{4,12},{8,0},{12,4},{1,9},{5,13},{9,1},{13,5},{2,10},{6,14},... | collective-permute-start | bytes 3080 | tf_op jit(solution)/shard_map/ppermute | solution.py:36
  128.6 4.6 %collective-permute-start.11 = (f32[2,4,32]{2,1,0:T(4,128)S(1)}, f32[2,4,32]{2,1,0:T(4,128)S(1)}, u32[]{:S(2)}, u32[]{:S(2)}) collective-permute-start(f32[2,4,32]{2,1,0:T(4,128)S(1)} %fusion.103), channel_id=1, source_target_pairs={{0,1},{1,0},{2,3},{3,2},{4,5},{5,4},{6,7},{7,6},{8,9},{9,8},{10,11... | collective-permute-start | bytes 3080 | tf_op jit(solution)/shard_map/ppermute | solution.py:36
  133.2 6.1 %collective-permute-start.12 = (f32[2,4,32]{2,1,0:T(4,128)S(1)}, f32[2,4,32]{2,1,0:T(4,128)S(1)}, u32[]{:S(2)}, u32[]{:S(2)}) collective-permute-start(f32[2,4,32]{2,1,0:T(4,128)S(1)} %add.132), channel_id=1, source_target_pairs={{0,2},{1,3},{2,0},{3,1},{4,6},{5,7},{6,4},{7,5},{8,10},{9,11},{10,... | collective-permute-start | bytes 3080 | tf_op jit(solution)/shard_map/ppermute | solution.py:36
Sparse Core Ops, SparseCore 0:
  10.3 64.2 all-gather.2
  140.2 73.7 all-gather.4
where the time goes:
time: 234 us; the launch traced here: 233 us
  waiting for transfers between devices  123 us (53%)
  starting transfers between devices  59.3 us (25%)
  matrix products  24.5 us (10%)
  between operations  13.8 us (6%)
  other arithmetic  7.72 us (3%)
  local copies, waits for them, and re-layouts  5.18 us (2%)
    all_gather x1, waiting for transfers between devices, body(): lax.all_gather(big, 'tm', axis=0, tiled=True).reshape(ranks, 8, 1024)  73.9 us
    ppermute x8, starting transfers between devices, butterfly_sum(): x = x + lax.ppermute(x, axis, pairs)  29.9 us
    all_gather x1, waiting for transfers between devices, body(): gathered = lax.all_gather(packed, ('band', 'fsdp'), axis=0, tiled=True)  23.3 us
    all_to_all x1, starting transfers between devices, body(): lax.all_to_all(flat_resid, 'tm', split_axis=0, concat_axis=0, tiled=True)  15.1 us
    ppermute x8, waiting for transfers between devices, butterfly_sum(): x = x + lax.ppermute(x, axis, pairs)  12 us
    ppermute x2, waiting for transfers between devices, with_halo(): after = lax.ppermute(initial, axis, down)  7.84 us
    ppermute x2, starting transfers between devices, with_halo(): before = lax.ppermute(last, axis, up)  6.45 us
    dot_general x9, matrix products, body(): jnp.einsum('fhwc,cd->fhwd', padded[:, shift_y:shift_y + height, shift_x:s...  5.7 us
  transfers between devices with their start and end apart: 16, of which 14 were waited for; matrix products, arithmetic and copies ran while one was open for 4% of the time, Pallas kernels for 0%

commit v1 on v0

--- a/solution.py
+++ b/solution.py
@@ -3,6 +3,7 @@
 import jax.numpy as jnp
 from jax import lax
 from jax.sharding import PartitionSpec as P
+from jax.lax import all_to_all, axis_size
 
 GROUPS = 32
 EPS = 1e-06
@@ -123,9 +124,9 @@
     mean_two, scale_two = group_moments(resid)
     mine = jnp.concatenate([mean_two, scale_two], axis=1)
     big = jnp.pad(mine, ((0, 8 - frames), (0, 1024 - 2 * GROUPS)))
-    moments = lax.all_gather(big, "tm", axis=0, tiled=True).reshape(ranks, 8, 1024)[
-        :, :frames, : 2 * GROUPS
-    ]
+    moments = jnp.concatenate(
+        all_to_all(jnp.stack([big] * axis_size("tm")), "tm", 0, 0), axis=0
+    ).reshape(ranks, 8, 1024)[:, :frames, : 2 * GROUPS]
     moments = moments.reshape(total_frames, 2 * GROUPS)
     mean_all, scale_all = (moments[:, :GROUPS], moments[:, GROUPS:])
     flat_norm = apply_norm(resid_time, mean_all, scale_all, norm_gains[1]).astype(jnp.bfloat16)

time: 234 us -> 255 us (1.090)
  waiting for transfers between devices: 123 us -> 138 us
  starting transfers between devices: 59.3 us -> 64 us
    all_gather x1 -> x0, waiting for transfers between devices: 73.9 us -> none  [body(): lax.all_gather(big, 'tm', axis=0, tiled=True).reshape(ranks, 8, 1024)]
    all_to_all x0 -> x1, waiting for transfers between devices: none -> 55.4 us  [body(): all_to_all(jnp.stack([big] * axis_size('tm')), 'tm', 0, 0)]
    all_to_all x1, waiting for transfers between devices: 0.01 us -> 33.6 us  [body(): lax.all_to_all(flat_resid, 'tm', split_axis=0, concat_axis=0, tiled=True)]
    all_to_all x0 -> x1, starting transfers between devices: none -> 4.76 us  [body(): all_to_all(jnp.stack([big] * axis_size('tm')), 'tm', 0, 0)]
  transfers between devices with their start and end apart: 16 -> 16, of which waited for: 14 -> 15; matrix products, arithmetic and copies ran while one was open for 4% -> 3% of each run, Pallas kernels for 0% -> 0%
where the time goes in v1:
time: 255 us; the launch traced here: 254 us
  waiting for transfers between devices  138 us (54%)
  starting transfers between devices  64 us (25%)
  matrix products  24.5 us (10%)
  between operations  13.8 us (5%)
  other arithmetic  7.12 us (3%)
  local copies, waits for them, and re-layouts  6.26 us (2%)
    all_to_all x1, waiting for transfers between devices, body(): all_to_all(jnp.stack([big] * axis_size('tm')), 'tm', 0, 0)  55.4 us
    all_to_all x1, waiting for transfers between devices, body(): lax.all_to_all(flat_resid, 'tm', split_axis=0, concat_axis=0, tiled=True)  33.6 us
    ppermute x8, starting transfers between devices, butterfly_sum(): x = x + lax.ppermute(x, axis, pairs)  29.9 us
    all_gather x1, waiting for transfers between devices, body(): gathered = lax.all_gather(packed, ('band', 'fsdp'), axis=0, tiled=True)  23.3 us
    all_to_all x1, starting transfers between devices, body(): lax.all_to_all(flat_resid, 'tm', split_axis=0, concat_axis=0, tiled=True)  15.1 us
    ppermute x8, waiting for transfers between devices, butterfly_sum(): x = x + lax.ppermute(x, axis, pairs)  12 us
    ppermute x2, waiting for transfers between devices, with_halo(): after = lax.ppermute(initial, axis, down)  7.84 us
    ppermute x2, starting transfers between devices, with_halo(): before = lax.ppermute(last, axis, up)  6.45 us
  transfers between devices with their start and end apart: 16, of which 15 were waited for; matrix products, arithmetic and copies ran while one was open for 3% of the time, Pallas kernels for 0%

profile of v1, /device:TPU:1, one launch (start us, length us, event | category | flops | bytes accessed | tf_op | source)
XLA Modules:
  0.0 253.6 jit_solution(450490602949746780)
XLA Ops:
  6.5 1.7 pad_maximum_fusion.2
  8.3 1.5 convert_reduce_fusion
  10.2 4.0 %collective-permute-start = (f32[2,4,32]{2,1,0:T(4,128)S(1)}, f32[2,4,32]{2,1,0:T(4,128)S(1)}, u32[]{:S(2)}, u32[]{:S(2)}) collective-permute-start(f32[2,4,32]{2,1,0:T(4,128)S(1)} %pad_maximum_fusion.6), channel_id=1, source_target_pairs={{0,4},{4,0},{8,12},{12,8},{1,5},{5,1},{9,13},{13,9},{2,6},{6,2},{1... | collective-permute-start | bytes 3080 | tf_op jit(solution)/shard_map/ppermute | solution.py:37
  14.2 1.0 collective-permute-done
  15.2 5.0 %collective-permute-start.1 = (f32[2,4,32]{2,1,0:T(4,128)S(1)}, f32[2,4,32]{2,1,0:T(4,128)S(1)}, u32[]{:S(2)}, u32[]{:S(2)}) collective-permute-start(f32[2,4,32]{2,1,0:T(4,128)S(1)} %fusion.93), channel_id=1, source_target_pairs={{0,8},{4,12},{8,0},{12,4},{1,9},{5,13},{9,1},{13,5},{2,10},{6,14},... | collective-permute-start | bytes 3080 | tf_op jit(solution)/shard_map/ppermute | solution.py:37
  20.2 1.0 collective-permute-done.1
  21.2 3.2 %collective-permute-start.2 = (f32[2,4,32]{2,1,0:T(4,128)S(1)}, f32[2,4,32]{2,1,0:T(4,128)S(1)}, u32[]{:S(2)}, u32[]{:S(2)}) collective-permute-start(f32[2,4,32]{2,1,0:T(4,128)S(1)} %fusion.104), channel_id=1, source_target_pairs={{0,1},{1,0},{2,3},{3,2},{4,5},{5,4},{6,7},{7,6},{8,9},{9,8},{10,11... | collective-permute-start | bytes 3080 | tf_op jit(solution)/shard_map/ppermute | solution.py:37
  24.3 1.2 collective-permute-done.2
  25.5 4.7 %collective-permute-start.3 = (f32[2,4,32]{2,1,0:T(4,128)S(1)}, f32[2,4,32]{2,1,0:T(4,128)S(1)}, u32[]{:S(2)}, u32[]{:S(2)}) collective-permute-start(f32[2,4,32]{2,1,0:T(4,128)S(1)} %add.111), channel_id=1, source_target_pairs={{0,2},{1,3},{2,0},{3,1},{4,6},{5,7},{6,4},{7,5},{8,10},{9,11},{10,... | collective-permute-start | bytes 3080 | tf_op jit(solution)/shard_map/ppermute | solution.py:37
  30.2 0.8 fusion.96
  31.8 0.7 fusion.16
  32.4 3.2 %collective-permute-start.4 = (bf16[4,1,32,256]{3,2,1,0:T(8,128)(2,1)S(1)}, bf16[4,1,32,256]{3,2,1,0:T(8,128)(2,1)S(1)}, u32[]{:S(2)}, u32[]{:S(2)}) collective-permute-start(bf16[4,1,32,256]{3,2,1,0:T(8,128)(2,1)S(1)} %get-tuple-element.13), channel_id=1, source_target_pairs={{0,4},{4,8},{8,12},{1,5},{5,9},{9,13},{2,6},{6,10},{10,14},{3,7},{... | collective-permute-start | bytes 196616 | tf_op jit(solution)/shard_map/ppermute | solution.py:19
  35.7 1.3 collective-permute-start.5
  37.0 4.1 %collective-permute-done.5 = bf16[4,1,32,256]{3,2,1,0:T(8,128)(2,1)S(1)} collective-permute-done((bf16[4,1,32,256]{3,2,1,0:T(8,128)(2,1)S(1)}, bf16[4,1,32,256]{3,2,1,0:T(8,128)(2,1)S(1)}, u32[]{:S(2)}, u32[]{:S(2)}) %collective-permute-start.5) | collective-permute-done | bytes 65568 | tf_op jit(solution)/shard_map/ppermute | solution.py:20
  41.3 3.2 %collective-permute-start.6 = (bf16[4,18,1,256]{3,2,1,0:T(2,128)(2,1)S(1)}, bf16[4,18,1,256]{3,2,1,0:T(2,128)(2,1)S(1)}, u32[]{:S(2)}, u32[]{:S(2)}) collective-permute-start(bf16[4,18,1,256]{3,2,1,0:T(2,128)(2,1)S(1)} %get-tuple-element.12), channel_id=1, source_target_pairs={{0,1},{1,2},{2,3},{4,5},{5,6},{6,7},{8,9},{9,10},{10,11},{12,13},{... | collective-permute-start | bytes 110600 | tf_op jit(solution)/shard_map/ppermute | solution.py:19
  44.5 1.3 collective-permute-start.7
  45.9 3.7 %collective-permute-done.7 = bf16[4,18,1,256]{3,2,1,0:T(2,128)(2,1)S(1)} collective-permute-done((bf16[4,18,1,256]{3,2,1,0:T(2,128)(2,1)S(1)}, bf16[4,18,1,256]{3,2,1,0:T(2,128)(2,1)S(1)}, u32[]{:S(2)}, u32[]{:S(2)}) %collective-permute-start.7) | collective-permute-done | bytes 36896 | tf_op jit(solution)/shard_map/ppermute | solution.py:20
  49.6 1.8 pad_maximum_fusion.1
  51.3 23.3 %all-gather.2.cloned.1.call-done = bf16[256,4096]{1,0:T(8,128)(2,1)} async-done(((bf16[16,4096]{1,0:T(8,128)(2,1)}), bf16[256,4096]{1,0:T(8,128)(2,1)}) %all-gather.2.cloned.1.call-update) | async-done | bytes 2097168 | tf_op jit(solution)/shard_map/all_gather | solution.py:77
  74.7 1.5 fusion.51
  76.8 0.9 copy-done
  80.4 1.1 add_convert_fusion
  81.5 5.3 %collective-permute-start.8 = (bf16[2,16,32,256]{3,2,1,0:T(8,128)(2,1)S(1)}, bf16[2,16,32,256]{3,2,1,0:T(8,128)(2,1)S(1)}, u32[]{:S(2)}, u32[]{:S(2)}) collective-permute-start(bf16[2,16,32,256]{3,2,1,0:T(8,128)(2,1)S(1)} %slice.197), channel_id=1, source_target_pairs={{0,16},{16,32},{32,48},{48,64},{64,80},{80,96},{96,112},{112,128},... | collective-permute-start | bytes 1572872 | tf_op jit(solution)/shard_map/ppermute | solution.py:28
  87.2 5.7 %collective-permute-done.8 = bf16[2,16,32,256]{3,2,1,0:T(8,128)(2,1)S(1)} collective-permute-done((bf16[2,16,32,256]{3,2,1,0:T(8,128)(2,1)S(1)}, bf16[2,16,32,256]{3,2,1,0:T(8,128)(2,1)S(1)}, u32[]{:S(2)}, u32[]{:S(2)}) %collective-permute-start.8) | collective-permute-done | bytes 524320 | tf_op jit(solution)/shard_map/ppermute | solution.py:28
  93.0 1.2 fusion.22
  94.2 1.2 fusion.19
  95.4 1.2 fusion.25
  96.6 1.3 fusion.60
  98.0 1.4 fusion.62
  99.4 1.7 convert_reduce_fusion.1
  101.2 1.1 copy.99
  102.3 15.1 %all-to-all-start = ((bf16[32,4,16,256]{3,2,1,0:T(8,128)(2,1)}), bf16[32,4,16,256]{3,2,1,0:T(8,128)(2,1)S(1)}, u32[]{:S(2)}, u32[]{:S(2)}) async-start(bf16[32,4,16,256]{3,2,1,0:T(8,128)(2,1)} %bitcast.134), calls=%async_computation | async-start | bytes 2097152 | tf_op jit(solution)/shard_map/all_to_all | solution.py:122
  117.8 2.8 %collective-permute-start.9 = (f32[2,4,32]{2,1,0:T(4,128)S(1)}, f32[2,4,32]{2,1,0:T(4,128)S(1)}, u32[]{:S(2)}, u32[]{:S(2)}) collective-permute-start(f32[2,4,32]{2,1,0:T(4,128)S(1)} %pad_maximum_fusion.7), channel_id=1, source_target_pairs={{0,4},{4,0},{8,12},{12,8},{1,5},{5,1},{9,13},{13,9},{2,6},{6,2},{1... | collective-permute-start | bytes 3080 | tf_op jit(solution)/shard_map/ppermute | solution.py:37
  120.6 1.8 collective-permute-done.9
  122.4 3.7 %collective-permute-start.10 = (f32[2,4,32]{2,1,0:T(4,128)S(1)}, f32[2,4,32]{2,1,0:T(4,128)S(1)}, u32[]{:S(2)}, u32[]{:S(2)}) collective-permute-start(f32[2,4,32]{2,1,0:T(4,128)S(1)} %fusion.92), channel_id=1, source_target_pairs={{0,8},{4,12},{8,0},{12,4},{1,9},{5,13},{9,1},{13,5},{2,10},{6,14},... | collective-permute-start | bytes 3080 | tf_op jit(solution)/shard_map/ppermute | solution.py:37
  126.1 2.4 collective-permute-done.10
  128.6 2.8 %collective-permute-start.11 = (f32[2,4,32]{2,1,0:T(4,128)S(1)}, f32[2,4,32]{2,1,0:T(4,128)S(1)}, u32[]{:S(2)}, u32[]{:S(2)}) collective-permute-start(f32[2,4,32]{2,1,0:T(4,128)S(1)} %fusion.103), channel_id=1, source_target_pairs={{0,1},{1,0},{2,3},{3,2},{4,5},{5,4},{6,7},{7,6},{8,9},{9,8},{10,11... | collective-permute-start | bytes 3080 | tf_op jit(solution)/shard_map/ppermute | solution.py:37
  131.3 1.8 collective-permute-done.11
  133.2 3.7 %collective-permute-start.12 = (f32[2,4,32]{2,1,0:T(4,128)S(1)}, f32[2,4,32]{2,1,0:T(4,128)S(1)}, u32[]{:S(2)}, u32[]{:S(2)}) collective-permute-start(f32[2,4,32]{2,1,0:T(4,128)S(1)} %add.132), channel_id=1, source_target_pairs={{0,2},{1,3},{2,0},{3,1},{4,6},{5,7},{6,4},{7,5},{8,10},{9,11},{10,... | collective-permute-start | bytes 3080 | tf_op jit(solution)/shard_map/ppermute | solution.py:37
  136.9 2.4 collective-permute-done.12
  139.4 33.6 %all-to-all-done = bf16[32,4,16,256]{3,2,1,0:T(8,128)(2,1)S(1)} async-done(((bf16[32,4,16,256]{3,2,1,0:T(8,128)(2,1)}), bf16[32,4,16,256]{3,2,1,0:T(8,128)(2,1)S(1)}, u32[]{:S(2)}, u32[]{:S(2)}) %all-to-all-start) | async-done | bytes 1048608 | tf_op jit(solution)/shard_map/all_to_all | solution.py:122
  173.1 1.1 stack.20
  174.1 4.8 %all-to-all-start.1 = ((f32[32,8,1024]{2,1,0:T(8,128)}), f32[32,8,1024]{2,1,0:T(8,128)}, u32[]{:S(2)}, u32[]{:S(2)}) async-start(f32[32,8,1024]{2,1,0:T(8,128)} %stack.20), calls=%async_computation.1 | async-start | bytes 2097152 | tf_op jit(solution)/shard_map/all_to_all | solution.py:128
  179.3 55.4 %all-to-all-done.1 = f32[32,8,1024]{2,1,0:T(8,128)} async-done(((f32[32,8,1024]{2,1,0:T(8,128)}), f32[32,8,1024]{2,1,0:T(8,128)}, u32[]{:S(2)}, u32[]{:S(2)}) %all-to-all-start.1) | async-done | bytes 1048608 | tf_op jit(solution)/shard_map/all_to_all | solution.py:128
  234.7 0.9 slice.203
  236.1 4.6 %convolution_convert_fusion = bf16[128,16,768]{2,0,1:T(8,128)(2,1)} fusion(f32[128,16,256]{2,1,0:T(8,128)S(1)} %bitcast_convert_fusion, f32[256]{0:T(256)S(1)} %bitcast.149, f32[128,256]{1,0:T(8,128)S(1)} %copy.54, f32[128,256]{1,0:T(8,128)S(1)} %copy.52, bf16[256,4096]{1,0:T(8,128)(2,1)} %all-gather.2.cloned.1.call-done), kind=kOutput, calls=%fused_computation.7 | convolution fusion | flops 808976384 | bytes 5899264 | tf_op jit(solution)/shard_map/fpc,cd->fpd/dot_general | solution.py:133
  240.8 2.1 fusion.97
  242.9 3.9 %fusion.31 = bf16[1,1,16,128,256]{4,3,2,1,0:T(8,128)(2,1)} fusion(f32[128,16,256]{2,1,0:T(8,128)S(1)} %bitcast_convert_fusion, bf16[128,16,768]{2,0,1:T(8,128)(2,1)} %convolution_convert_fusion, f32[16,128,128]{1,2,0:T(8,128)S(1)} %get-tuple-element.24, f32[16,128]{1,0:T(8,128)S(1)} %get-tuple-element.23, bf16[256,4096]{1,0:T(8,128)(2,1)} %all-gather.2.cloned.1.call-done), kind=kOutput, calls=%fused_computation.39 | convolution fusion | flops 404750336 | bytes 5382144 | tf_op jit(solution)/shard_map/axi,iy->axy/dot_general | solution.py:151
  (67 shorter events, 6.6 us)
Async XLA Ops:
  6.5 25.2 %copy-start.1 = (bf16[4,16,32,256]{3,2,1,0:T(8,128)(2,1)S(1)}, bf16[4,16,32,256]{3,2,1,0:T(8,128)(2,1)}, u32[]{:S(2)}) copy-start(bf16[4,16,32,256]{3,2,1,0:T(8,128)(2,1)} %param.7) | copy-start | bytes 3145732
  6.5 68.1 %all-gather.2.cloned.1.call-start = ((), (), s32[]{:S(2)}) async-start(), calls=%async_computation.2 | async-start | bytes 2228224 | tf_op jit(solution)/shard_map/all_gather | solution.py:77
  10.2 5.0 %collective-permute-start = (f32[2,4,32]{2,1,0:T(4,128)S(1)}, f32[2,4,32]{2,1,0:T(4,128)S(1)}, u32[]{:S(2)}, u32[]{:S(2)}) collective-permute-start(f32[2,4,32]{2,1,0:T(4,128)S(1)} %pad_maximum_fusion.6), channel_id=1, source_target_pairs={{0,4},{4,0},{8,12},{12,8},{1,5},{5,1},{9,13},{13,9},{2,6},{6,2},{1... | collective-permute-start | bytes 3080 | tf_op jit(solution)/shard_map/ppermute | solution.py:37
  15.2 6.0 %collective-permute-start.1 = (f32[2,4,32]{2,1,0:T(4,128)S(1)}, f32[2,4,32]{2,1,0:T(4,128)S(1)}, u32[]{:S(2)}, u32[]{:S(2)}) collective-permute-start(f32[2,4,32]{2,1,0:T(4,128)S(1)} %fusion.93), channel_id=1, source_target_pairs={{0,8},{4,12},{8,0},{12,4},{1,9},{5,13},{9,1},{13,5},{2,10},{6,14},... | collective-permute-start | bytes 3080 | tf_op jit(solution)/shard_map/ppermute | solution.py:37
  21.2 4.3 %collective-permute-start.2 = (f32[2,4,32]{2,1,0:T(4,128)S(1)}, f32[2,4,32]{2,1,0:T(4,128)S(1)}, u32[]{:S(2)}, u32[]{:S(2)}) collective-permute-start(f32[2,4,32]{2,1,0:T(4,128)S(1)} %fusion.104), channel_id=1, source_target_pairs={{0,1},{1,0},{2,3},{3,2},{4,5},{5,4},{6,7},{7,6},{8,9},{9,8},{10,11... | collective-permute-start | bytes 3080 | tf_op jit(solution)/shard_map/ppermute | solution.py:37
  25.5 5.8 %collective-permute-start.3 = (f32[2,4,32]{2,1,0:T(4,128)S(1)}, f32[2,4,32]{2,1,0:T(4,128)S(1)}, u32[]{:S(2)}, u32[]{:S(2)}) collective-permute-start(f32[2,4,32]{2,1,0:T(4,128)S(1)} %add.111), channel_id=1, source_target_pairs={{0,2},{1,3},{2,0},{3,1},{4,6},{5,7},{6,4},{7,5},{8,10},{9,11},{10,... | collective-permute-start | bytes 3080 | tf_op jit(solution)/shard_map/ppermute | solution.py:37
  32.4 4.6 %collective-permute-start.4 = (bf16[4,1,32,256]{3,2,1,0:T(8,128)(2,1)S(1)}, bf16[4,1,32,256]{3,2,1,0:T(8,128)(2,1)S(1)}, u32[]{:S(2)}, u32[]{:S(2)}) collective-permute-start(bf16[4,1,32,256]{3,2,1,0:T(8,128)(2,1)S(1)} %get-tuple-element.13), channel_id=1, source_target_pairs={{0,4},{4,8},{8,12},{1,5},{5,9},{9,13},{2,6},{6,10},{10,14},{3,7},{... | collective-permute-start | bytes 196616 | tf_op jit(solution)/shard_map/ppermute | solution.py:19
  35.7 5.4 %collective-permute-start.5 = (bf16[4,1,32,256]{3,2,1,0:T(8,128)(2,1)S(1)}, bf16[4,1,32,256]{3,2,1,0:T(8,128)(2,1)S(1)}, u32[]{:S(2)}, u32[]{:S(2)}) collective-permute-start(bf16[4,1,32,256]{3,2,1,0:T(8,128)(2,1)S(1)} %get-tuple-element.14), channel_id=1, source_target_pairs={{4,0},{8,4},{12,8},{5,1},{9,5},{13,9},{6,2},{10,6},{14,10},{7,3},{... | collective-permute-start | bytes 196616 | tf_op jit(solution)/shard_map/ppermute | solution.py:20
  41.3 4.6 %collective-permute-start.6 = (bf16[4,18,1,256]{3,2,1,0:T(2,128)(2,1)S(1)}, bf16[4,18,1,256]{3,2,1,0:T(2,128)(2,1)S(1)}, u32[]{:S(2)}, u32[]{:S(2)}) collective-permute-start(bf16[4,18,1,256]{3,2,1,0:T(2,128)(2,1)S(1)} %get-tuple-element.12), channel_id=1, source_target_pairs={{0,1},{1,2},{2,3},{4,5},{5,6},{6,7},{8,9},{9,10},{10,11},{12,13},{... | collective-permute-start | bytes 110600 | tf_op jit(solution)/shard_map/ppermute | solution.py:19
  44.5 5.1 %collective-permute-start.7 = (bf16[4,18,1,256]{3,2,1,0:T(2,128)(2,1)S(1)}, bf16[4,18,1,256]{3,2,1,0:T(2,128)(2,1)S(1)}, u32[]{:S(2)}, u32[]{:S(2)}) collective-permute-start(bf16[4,18,1,256]{3,2,1,0:T(2,128)(2,1)S(1)} %get-tuple-element.11), channel_id=1, source_target_pairs={{1,0},{2,1},{3,2},{5,4},{6,5},{7,6},{9,8},{10,9},{11,10},{13,12},{... | collective-permute-start | bytes 110600 | tf_op jit(solution)/shard_map/ppermute | solution.py:20
  74.6 1.7 copy-start.3
  76.3 1.4 copy-start
  80.4 6.4 %copy-start.4 = (s32[16]{0:T(128)S(1)}, s32[16]{0:T(128)}, u32[]{:S(2)}) copy-start(s32[16]{0:T(128)} %param.8) | copy-start | bytes 196
  81.5 11.4 %collective-permute-start.8 = (bf16[2,16,32,256]{3,2,1,0:T(8,128)(2,1)S(1)}, bf16[2,16,32,256]{3,2,1,0:T(8,128)(2,1)S(1)}, u32[]{:S(2)}, u32[]{:S(2)}) collective-permute-start(bf16[2,16,32,256]{3,2,1,0:T(8,128)(2,1)S(1)} %slice.197), channel_id=1, source_target_pairs={{0,16},{16,32},{32,48},{48,64},{64,80},{80,96},{96,112},{112,128},... | collective-permute-start | bytes 1572872 | tf_op jit(solution)/shard_map/ppermute | solution.py:28
  98.0 1.4 copy-start.2
  102.3 70.8 %all-to-all-start = ((bf16[32,4,16,256]{3,2,1,0:T(8,128)(2,1)}), bf16[32,4,16,256]{3,2,1,0:T(8,128)(2,1)S(1)}, u32[]{:S(2)}, u32[]{:S(2)}) async-start(bf16[32,4,16,256]{3,2,1,0:T(8,128)(2,1)} %bitcast.134), calls=%async_computation | async-start | bytes 2097152 | tf_op jit(solution)/shard_map/all_to_all | solution.py:122
  117.8 4.6 %collective-permute-start.9 = (f32[2,4,32]{2,1,0:T(4,128)S(1)}, f32[2,4,32]{2,1,0:T(4,128)S(1)}, u32[]{:S(2)}, u32[]{:S(2)}) collective-permute-start(f32[2,4,32]{2,1,0:T(4,128)S(1)} %pad_maximum_fusion.7), channel_id=1, source_target_pairs={{0,4},{4,0},{8,12},{12,8},{1,5},{5,1},{9,13},{13,9},{2,6},{6,2},{1... | collective-permute-start | bytes 3080 | tf_op jit(solution)/shard_map/ppermute | solution.py:37
  122.4 6.1 %collective-permute-start.10 = (f32[2,4,32]{2,1,0:T(4,128)S(1)}, f32[2,4,32]{2,1,0:T(4,128)S(1)}, u32[]{:S(2)}, u32[]{:S(2)}) collective-permute-start(f32[2,4,32]{2,1,0:T(4,128)S(1)} %fusion.92), channel_id=1, source_target_pairs={{0,8},{4,12},{8,0},{12,4},{1,9},{5,13},{9,1},{13,5},{2,10},{6,14},... | collective-permute-start | bytes 3080 | tf_op jit(solution)/shard_map/ppermute | solution.py:37
  128.6 4.6 %collective-permute-start.11 = (f32[2,4,32]{2,1,0:T(4,128)S(1)}, f32[2,4,32]{2,1,0:T(4,128)S(1)}, u32[]{:S(2)}, u32[]{:S(2)}) collective-permute-start(f32[2,4,32]{2,1,0:T(4,128)S(1)} %fusion.103), channel_id=1, source_target_pairs={{0,1},{1,0},{2,3},{3,2},{4,5},{5,4},{6,7},{7,6},{8,9},{9,8},{10,11... | collective-permute-start | bytes 3080 | tf_op jit(solution)/shard_map/ppermute | solution.py:37
  133.2 6.1 %collective-permute-start.12 = (f32[2,4,32]{2,1,0:T(4,128)S(1)}, f32[2,4,32]{2,1,0:T(4,128)S(1)}, u32[]{:S(2)}, u32[]{:S(2)}) collective-permute-start(f32[2,4,32]{2,1,0:T(4,128)S(1)} %add.132), channel_id=1, source_target_pairs={{0,2},{1,3},{2,0},{3,1},{4,6},{5,7},{6,4},{7,5},{8,10},{9,11},{10,... | collective-permute-start | bytes 3080 | tf_op jit(solution)/shard_map/ppermute | solution.py:37
  174.1 60.6 %all-to-all-start.1 = ((f32[32,8,1024]{2,1,0:T(8,128)}), f32[32,8,1024]{2,1,0:T(8,128)}, u32[]{:S(2)}, u32[]{:S(2)}) async-start(f32[32,8,1024]{2,1,0:T(8,128)} %stack.20), calls=%async_computation.1 | async-start | bytes 2097152 | tf_op jit(solution)/shard_map/all_to_all | solution.py:128
Sparse Core Ops, SparseCore 0:
  10.3 64.2 all-gather.1
